TPU v7x, 32 devices: a whole 2x2x4 slice. The times are simulated.
32 devices in a mesh: ri: 4 (over z), ao: 8 (over y, x, core).
Axes of the slice: x: 2, y: 2, z: 4, core: 2. Of those that a mesh axis runs over, the one named last changes fastest.
Arguments:
- tensor: bfloat16 [512, 256, 256], P('ri', 'ao'), may hold values from -0.5 to 0.5
- live_blocks: int32 [8, 8, 8], P('ri', 'ao'), may hold values 0 or 1
- occ_density: bfloat16 [256, 256], P('ao'), may hold values from -0.375 to 0.375
- virt_density: bfloat16 [256, 256], P('ao'), may hold values from -0.375 to 0.375
- occ_mask: int32 [8, 8], P('ao'), may hold values 0 or 1
- virt_mask: int32 [8, 8], P('ao'), may hold values 0 or 1
- pair_slots: int32 [8, 8], P('ao'), may hold values from 0 to 7, as said below
Outputs:
- polar: float32 [512, 512], P('ri', 'ao')
Inputs may be any that keep to these rules, and one draw needn't show every extreme that they name: pair_slots[b, 0] = b, and the 8 entries of a row are different AO blocks.
All inputs are finite; a program needn't handle non-finite values. No bound on the sum of `live_blocks` or of `occ_mask` or of `virt_mask` on one device may be relied on, other than what follows from the above.
Results may differ from a plain program's by a relative error of at most 0.0041.
Values may be sent and summed in bfloat16 or wider, within the bound.
No kernel may reach another device: no remote copies, remote signals or barrier semaphores. Data moves between devices by JAX's collectives and lax.ppermute only.
A program may use at most 192 MiB of HBM per device.

v0:
```python
import jax
import jax.numpy as jnp
from jax import lax
from jax.sharding import PartitionSpec as P

BS = 32
KS = 8
RB = 64


def shifted(block, axis, distance):
    devices = range(lax.axis_size(axis))
    route = [((i - distance) % len(devices), i) for i in devices]
    return lax.ppermute(block, axis, route)


def screen_density(density, block_mask):
    own_blocks = block_mask.shape[0]
    all_blocks = block_mask.shape[1]
    shaped = density.reshape(own_blocks, BS, all_blocks, BS)
    keeper = block_mask.astype(density.dtype)[:, None, :, None]
    return (shaped * keeper).reshape(density.shape)


def pick_slots(pair_slots, stacked, first_block):
    own_blocks = stacked.shape[1] // BS
    block_ids = first_block + jnp.arange(own_blocks, dtype=jnp.int32)
    matches = (pair_slots[:, :, None] == block_ids[None, None, :]).astype(jnp.bfloat16)
    shaped = stacked.reshape(2, own_blocks, BS, stacked.shape[2])
    return jnp.einsum("bkc,tcjn->tbkjn", matches, shaped, preferred_element_type=jnp.float32)


def per_device(tensor, live_blocks, occ_density, virt_density, occ_mask, virt_mask, pair_slots):
    own_rows = tensor.shape[0]
    own_width = tensor.shape[1]
    own_blocks = own_width // BS
    groups = live_blocks.shape[0]
    keeper = live_blocks.astype(jnp.bfloat16)[:, None, :, None, :, None]
    tensor_eff = (tensor.reshape(groups, RB, own_blocks, BS, KS, BS) * keeper).reshape(tensor.shape)
    stacked = jnp.stack(
        [screen_density(occ_density, occ_mask), screen_density(virt_density, virt_mask)]
    )
    ao_total = stacked.shape[2]
    cycle_size = lax.axis_size("ao")
    position = lax.axis_index("ao")

    def visit(turn_index, state):
        current, gathered_rows = state
        current = shifted(current, "ao", 1)
        source = (position - turn_index + cycle_size) % cycle_size
        return (current, gathered_rows + pick_slots(pair_slots, current, source * own_blocks))

    start_pick = pick_slots(pair_slots, stacked, position * own_blocks)
    unused, picked = lax.fori_loop(1, cycle_size, visit, (stacked, start_pick))
    picked = picked.astype(jnp.bfloat16)
    occ_rows = picked[0]
    virt_rows = picked[1]
    span_cols = min(128, ao_total)
    piece_count = ao_total // span_cols
    tensor_five = tensor_eff.reshape(own_rows, own_blocks, BS, KS, BS)
    occ_pieces = occ_rows.reshape(own_blocks, KS, BS, piece_count, span_cols)

    def occ_piece(piece_index):
        columns = lax.dynamic_index_in_dim(occ_pieces, piece_index, 3, keepdims=False)
        product = jnp.einsum(
            "pbikj,bkjl->lbip", tensor_five, columns, preferred_element_type=jnp.float32
        )
        return product.astype(jnp.bfloat16).reshape(span_cols, own_width, own_rows)

    half_occ = lax.map(occ_piece, jnp.arange(piece_count, dtype=jnp.int32)).reshape(
        ao_total, own_width, own_rows
    )
    half_occ_local = lax.all_to_all(half_occ, "ao", split_axis=0, concat_axis=1, tiled=True)

    def virt_piece(source_rows, piece_index):
        columns = lax.dynamic_slice_in_dim(virt_rows, piece_index * span_cols, span_cols, 3)
        product = jnp.einsum(
            "qbikj,bkjn->qbin", source_rows, columns, preferred_element_type=jnp.float32
        )
        return product.astype(jnp.bfloat16).reshape(source_rows.shape[0], own_width, span_cols)

    all_tensor = lax.all_gather(tensor_eff, "ri", axis=0, tiled=True)
    kept_rows = all_tensor.shape[0] // cycle_size
    source_rows = all_tensor
    polar_source_rows = source_rows.reshape(kept_rows * lax.axis_size("ao"), own_blocks, BS, KS, BS)

    def add_piece(piece_index, running):
        virt_part = virt_piece(polar_source_rows, piece_index)
        occ_part = lax.dynamic_slice_in_dim(half_occ_local, piece_index * span_cols, span_cols, 1)
        return running + jnp.einsum(
            "qln,lnp->qp", virt_part, occ_part, preferred_element_type=jnp.float32
        )

    polar_block = lax.psum_scatter(
        lax.fori_loop(
            0,
            piece_count,
            add_piece,
            jnp.zeros((polar_source_rows.shape[0], own_rows), jnp.float32),
        ),
        "ao",
        scatter_dimension=0,
        tiled=True,
    )
    return polar_block.T


def solution(mesh):
    placed = (
        P("ri", "ao", None),
        P("ri", "ao", None),
        P("ao", None),
        P("ao", None),
        P("ao", None),
        P("ao", None),
        P("ao", None),
    )
    return jax.shard_map(
        per_device, mesh=mesh, in_specs=placed, out_specs=P("ri", "ao"), check_vma=False
    )
```

profile of v0, /device:TPU:0, one launch (start us, length us, event | category | flops | bytes accessed | tf_op | source)
XLA Modules:
  0.0 228.5 jit_solution(457382478721264577)
XLA Ops:
  6.5 0.7 convert_element_type.41
  7.2 0.1 copy.51
  7.3 0.1 mul.93
  7.5 0.1 mul.94
  7.6 0.1 copy.41
  7.7 3.1 %broadcast_multiply_fusion.1 = bf16[128,32,256]{2,1,0:T(8,128)(2,1)} fusion(bf16[128,32,256]{2,1,0:T(8,128)(2,1)} %param.13, bf16[128,256]{1,0:T(8,128)(2,1)S(1)} %copy.41), kind=kLoop, calls=%fused_computation.23 | loop fusion | flops 1048576 | bytes 4259840 | tf_op jit(solution)/shard_map/mul | solution.py:39
  10.9 1.6 copy-done.1
  12.5 3.1 %copy.43 = bf16[128,32,256]{0,2,1:T(8,128)(2,1)} copy(bf16[128,32,256]{2,1,0:T(8,128)(2,1)S(1)} %copy-done.1) | data formatting | bytes 4194304 | tf_op args[0]
  16.0 0.1 multiply_bitcast_fusion
  16.1 32.0 %while.41 = (s32[]{:T(128)}, bf16[2,32,256]{2,1,0:T(8,128)(2,1)S(1)}, f32[2,1,8,32,256]{4,3,2,1,0:T(8,128)S(1)}, s32[]{:T(128)}, s32[1,8]{1,0:T(1,128)S(1)}, /*index=5*/s32[]{:T(128)}, s32[]{:T(128)}, s32[]{:T(128)}, s32[]{:T(128)}) while((s32[]{:T(128)}, bf16[2,32,256]{2,1,0:T(8,128)(2,1)S(1)}, f32[2,1,8,32,256]{4,3,2,1,0:T(8,128)S(1)}, ...), condition=%wide.region_1.2_spmd, body=%wide.region_0.1_spmd.sunk | while | flops 278559 | bytes 1409390 | solution.py:54
  16.1 0.5 collective-permute-start
  16.6 4.5 %collective-permute-done = bf16[2,32,256]{2,1,0:T(8,128)(2,1)S(1)} collective-permute-done((bf16[2,32,256]{2,1,0:T(8,128)(2,1)S(1)}, bf16[2,32,256]{2,1,0:T(8,128)(2,1)S(1)}, u32[]{:S(2)}, u32[]{:S(2)}) %collective-permute-start) | collective-permute-done | bytes 32800 | tf_op jit(solution)/shard_map/while/body/eval_jaxpr/ppermute | solution.py:14
  21.1 0.1 bitcast_add_fusion.2
  21.3 4.2 %collective-permute-done = bf16[2,32,256]{2,1,0:T(8,128)(2,1)S(1)} collective-permute-done((bf16[2,32,256]{2,1,0:T(8,128)(2,1)S(1)}, bf16[2,32,256]{2,1,0:T(8,128)(2,1)S(1)}, u32[]{:S(2)}, u32[]{:S(2)}) %collective-permute-start) | collective-permute-done | bytes 32800 | tf_op jit(solution)/shard_map/while/body/eval_jaxpr/ppermute | solution.py:14
  25.5 0.1 bitcast_add_fusion.2
  25.8 4.2 %collective-permute-done = bf16[2,32,256]{2,1,0:T(8,128)(2,1)S(1)} collective-permute-done((bf16[2,32,256]{2,1,0:T(8,128)(2,1)S(1)}, bf16[2,32,256]{2,1,0:T(8,128)(2,1)S(1)}, u32[]{:S(2)}, u32[]{:S(2)}) %collective-permute-start) | collective-permute-done | bytes 32800 | tf_op jit(solution)/shard_map/while/body/eval_jaxpr/ppermute | solution.py:14
  30.0 0.1 bitcast_add_fusion.2
  30.3 4.2 %collective-permute-done = bf16[2,32,256]{2,1,0:T(8,128)(2,1)S(1)} collective-permute-done((bf16[2,32,256]{2,1,0:T(8,128)(2,1)S(1)}, bf16[2,32,256]{2,1,0:T(8,128)(2,1)S(1)}, u32[]{:S(2)}, u32[]{:S(2)}) %collective-permute-start) | collective-permute-done | bytes 32800 | tf_op jit(solution)/shard_map/while/body/eval_jaxpr/ppermute | solution.py:14
  34.5 0.1 bitcast_add_fusion.2
  34.8 4.2 %collective-permute-done = bf16[2,32,256]{2,1,0:T(8,128)(2,1)S(1)} collective-permute-done((bf16[2,32,256]{2,1,0:T(8,128)(2,1)S(1)}, bf16[2,32,256]{2,1,0:T(8,128)(2,1)S(1)}, u32[]{:S(2)}, u32[]{:S(2)}) %collective-permute-start) | collective-permute-done | bytes 32800 | tf_op jit(solution)/shard_map/while/body/eval_jaxpr/ppermute | solution.py:14
  39.0 0.1 bitcast_add_fusion.2
  39.2 4.2 %collective-permute-done = bf16[2,32,256]{2,1,0:T(8,128)(2,1)S(1)} collective-permute-done((bf16[2,32,256]{2,1,0:T(8,128)(2,1)S(1)}, bf16[2,32,256]{2,1,0:T(8,128)(2,1)S(1)}, u32[]{:S(2)}, u32[]{:S(2)}) %collective-permute-start) | collective-permute-done | bytes 32800 | tf_op jit(solution)/shard_map/while/body/eval_jaxpr/ppermute | solution.py:14
  43.4 0.1 bitcast_add_fusion.2
  43.7 4.2 %collective-permute-done = bf16[2,32,256]{2,1,0:T(8,128)(2,1)S(1)} collective-permute-done((bf16[2,32,256]{2,1,0:T(8,128)(2,1)S(1)}, bf16[2,32,256]{2,1,0:T(8,128)(2,1)S(1)}, u32[]{:S(2)}, u32[]{:S(2)}) %collective-permute-start) | collective-permute-done | bytes 32800 | tf_op jit(solution)/shard_map/while/body/eval_jaxpr/ppermute | solution.py:14
  47.9 0.1 bitcast_add_fusion.2
  48.3 1.7 broadcast_multiply_fusion
  50.1 12.4 %while.42 = (s32[]{:T(128)}, bf16[2,128,32,128]{3,2,1,0:T(8,128)(2,1)}, s32[2]{0:T(128)S(1)}, bf16[1,8,32,2,128]{4,2,1,3,0:T(8,128)(2,1)S(1)}, bf16[128,1,32,8,3...) while((s32[]{:T(128)}, bf16[2,128,32,128]{3,2,1,0:T(8,128)(2,1)}, s32[2]{0:T(128)S(1)}, ...), condition=%wide.region_3.4_spmd, body=%wide.region_2.3_spmd.sunk | while | flops 268959744 | bytes 22085836 | solution.py:70
  50.1 0.6 dynamic_slice.40
  52.7 0.5 fusion.52
  53.1 1.1 copy-done.3
  54.3 0.7 copy_dynamic-update-slice_fusion.2
  55.0 1.3 copy-done.4
  56.3 0.6 dynamic_slice.40
  58.9 0.5 fusion.52
  59.3 1.1 copy-done.3
  60.4 0.7 copy_dynamic-update-slice_fusion.2
  61.2 1.3 copy-done.4
  62.5 3.6 %all-to-all-start = ((bf16[256,32,128]{2,1,0:T(8,128)(2,1)}), bf16[256,32,128]{2,1,0:T(8,128)(2,1)S(1)}, u32[]{:S(2)}, u32[]{:S(2)}) async-start(bf16[256,32,128]{2,1,0:T(8,128)(2,1)} %bitcast.132), calls=%async_computation | async-start | bytes 4194304 | tf_op jit(solution)/shard_map/all_to_all | solution.py:73
  66.2 26.5 %all-to-all-done = bf16[256,32,128]{2,1,0:T(8,128)(2,1)S(1)} async-done(((bf16[256,32,128]{2,1,0:T(8,128)(2,1)}), bf16[256,32,128]{2,1,0:T(8,128)(2,1)S(1)}, u32[]{:S(2)}, u32[]{:S(2)}) %all-to-all-start) | async-done | bytes 2097184 | tf_op jit(solution)/shard_map/all_to_all | solution.py:73
  92.7 1.3 copy-done.2
  94.0 2.2 copy.47
  96.3 67.1 %all-gather.2.cloned.1.call-done = bf16[512,32,256]{2,1,0:T(8,128)(2,1)} async-done(((bf16[128,32,256]{2,1,0:T(8,128)(2,1)}), bf16[512,32,256]{2,1,0:T(8,128)(2,1)}) %all-gather.2.cloned.1.call-update) | async-done | bytes 8388624 | tf_op jit(solution)/shard_map/all_gather | solution.py:82
  163.4 13.8 %copy.42 = bf16[512,32,256]{0,2,1:T(8,128)(2,1)} copy(bf16[512,32,256]{2,1,0:T(8,128)(2,1)} %all-gather.2.cloned.1.call-done) | data formatting | bytes 16777216 | tf_op jit(solution)/shard_map/all_gather | solution.py:82
  177.2 11.8 %while.43 = (s32[]{:T(128)}, f32[512,128]{1,0:T(8,128)S(1)}, bf16[1,8,32,256]{3,2,1,0:T(8,128)(2,1)S(1)}, bf16[512,1,32,8,32]{0,4,3,2,1:T(8,128)(2,1)}, bf16[32,...) while((s32[]{:T(128)}, f32[512,128]{1,0:T(8,128)S(1)}, ...), condition=%wide.region_5.6_spmd.clone, body=%wide.region_4.5_spmd.clone.sunk | while | flops 1612840960 | bytes 10028700 | solution.py:95
  177.2 5.9 %fusion.57 = f32[512,128]{1,0:T(8,128)S(1)} fusion(bf16[512,1,32,8,32]{0,4,3,2,1:T(8,128)(2,1)} %get-tuple-element.511, bf16[32,256,128]{2,1,0:T(8,128)(2,1)S(1)} %get-tuple-element.512, s32[]{:T(128)S(6)} %select_n.38, f32[512,128]{1,0:T(8,128)S(1)} %get-tuple-element.500, pred[]{:T(512)S(6)} %compare.4, ...), kind=kOutput, calls=%fused_computation.17.clone.1 | convolution fusion | flops 1612840960 | bytes 10028544 | tf_op jit(solution)/shard_map/while/body/eval_jaxpr/qln,lnp->qp/dot_general | solution.py:90
  183.1 5.9 %fusion.57 = f32[512,128]{1,0:T(8,128)S(1)} fusion(bf16[512,1,32,8,32]{0,4,3,2,1:T(8,128)(2,1)} %get-tuple-element.511, bf16[32,256,128]{2,1,0:T(8,128)(2,1)S(1)} %get-tuple-element.512, s32[]{:T(128)S(6)} %select_n.38, f32[512,128]{1,0:T(8,128)S(1)} %get-tuple-element.500, pred[]{:T(512)S(6)} %compare.4, ...), kind=kOutput, calls=%fused_computation.17.clone.1 | convolution fusion | flops 1612840960 | bytes 10028544 | tf_op jit(solution)/shard_map/while/body/eval_jaxpr/qln,lnp->qp/dot_general | solution.py:90
  189.0 0.7 copy-done
  189.7 32.0 %reduce-scatter.2.cloned.1.call-done = f32[64,128]{1,0:T(8,128)} async-done(((f32[512,128]{1,0:T(8,128)}), f32[64,128]{1,0:T(8,128)}) %reduce-scatter.2.cloned.1.call-update) | async-done | bytes 32784 | tf_op jit(solution)/shard_map/reduce_scatter | solution.py:94
  (66 shorter events, 1.2 us)
Async XLA Ops:
  6.5 156.8 %all-gather.2.cloned.1.call-start = ((), (), s32[]{:S(2)}) async-start(), calls=%async_computation.2 | async-start | bytes 10485760 | tf_op jit(solution)/shard_map/all_gather | solution.py:82
  10.8 1.6 copy-start.1
  12.4 3.1 %copy-start.7 = (s32[1,8]{1,0:T(1,128)S(1)}, s32[1,8]{1,0:T(1,128)}, u32[]{:S(2)}) copy-start(s32[1,8]{1,0:T(1,128)} %param.18) | copy-start | bytes 100
  12.4 3.3 %copy-start.8 = (s32[1,8]{1,0:T(1,128)S(1)}, s32[1,8]{1,0:T(1,128)}, u32[]{:S(2)}) copy-start(s32[1,8]{1,0:T(1,128)} %param.17) | copy-start | bytes 100
  12.4 3.5 %copy-start.5 = (bf16[32,256]{1,0:T(8,128)(2,1)S(1)}, bf16[32,256]{1,0:T(8,128)(2,1)}, u32[]{:S(2)}) copy-start(bf16[32,256]{1,0:T(8,128)(2,1)} %param.16) | copy-start | bytes 49156
  12.4 3.5 %copy-start.6 = (bf16[32,256]{1,0:T(8,128)(2,1)S(1)}, bf16[32,256]{1,0:T(8,128)(2,1)}, u32[]{:S(2)}) copy-start(bf16[32,256]{1,0:T(8,128)(2,1)} %param.15) | copy-start | bytes 49156
  12.4 3.5 %copy-start.9 = (s32[1,8]{1,0:T(1,128)S(1)}, s32[1,8]{1,0:T(1,128)}, u32[]{:S(2)}) copy-start(s32[1,8]{1,0:T(1,128)} %param.19) | copy-start | bytes 100
  16.1 5.0 %collective-permute-start = (bf16[2,32,256]{2,1,0:T(8,128)(2,1)S(1)}, bf16[2,32,256]{2,1,0:T(8,128)(2,1)S(1)}, u32[]{:S(2)}, u32[]{:S(2)}) collective-permute-start(bf16[2,32,256]{2,1,0:T(8,128)(2,1)S(1)} %get-tuple-element.449), channel_id=1, source_target_pairs={{7,0},{0,1},{1,2},{2,3},{3,4},{4,5},{5,6},{6,7},{15,8},{8,9},{9,10... | collective-permute-start | bytes 98312 | tf_op jit(solution)/shard_map/while/body/eval_jaxpr/ppermute | solution.py:14
  21.2 4.3 %collective-permute-start = (bf16[2,32,256]{2,1,0:T(8,128)(2,1)S(1)}, bf16[2,32,256]{2,1,0:T(8,128)(2,1)S(1)}, u32[]{:S(2)}, u32[]{:S(2)}) collective-permute-start(bf16[2,32,256]{2,1,0:T(8,128)(2,1)S(1)} %get-tuple-element.449), channel_id=1, source_target_pairs={{7,0},{0,1},{1,2},{2,3},{3,4},{4,5},{5,6},{6,7},{15,8},{8,9},{9,10... | collective-permute-start | bytes 98312 | tf_op jit(solution)/shard_map/while/body/eval_jaxpr/ppermute | solution.py:14
  25.7 4.3 %collective-permute-start = (bf16[2,32,256]{2,1,0:T(8,128)(2,1)S(1)}, bf16[2,32,256]{2,1,0:T(8,128)(2,1)S(1)}, u32[]{:S(2)}, u32[]{:S(2)}) collective-permute-start(bf16[2,32,256]{2,1,0:T(8,128)(2,1)S(1)} %get-tuple-element.449), channel_id=1, source_target_pairs={{7,0},{0,1},{1,2},{2,3},{3,4},{4,5},{5,6},{6,7},{15,8},{8,9},{9,10... | collective-permute-start | bytes 98312 | tf_op jit(solution)/shard_map/while/body/eval_jaxpr/ppermute | solution.py:14
  30.2 4.3 %collective-permute-start = (bf16[2,32,256]{2,1,0:T(8,128)(2,1)S(1)}, bf16[2,32,256]{2,1,0:T(8,128)(2,1)S(1)}, u32[]{:S(2)}, u32[]{:S(2)}) collective-permute-start(bf16[2,32,256]{2,1,0:T(8,128)(2,1)S(1)} %get-tuple-element.449), channel_id=1, source_target_pairs={{7,0},{0,1},{1,2},{2,3},{3,4},{4,5},{5,6},{6,7},{15,8},{8,9},{9,10... | collective-permute-start | bytes 98312 | tf_op jit(solution)/shard_map/while/body/eval_jaxpr/ppermute | solution.py:14
  34.7 4.3 %collective-permute-start = (bf16[2,32,256]{2,1,0:T(8,128)(2,1)S(1)}, bf16[2,32,256]{2,1,0:T(8,128)(2,1)S(1)}, u32[]{:S(2)}, u32[]{:S(2)}) collective-permute-start(bf16[2,32,256]{2,1,0:T(8,128)(2,1)S(1)} %get-tuple-element.449), channel_id=1, source_target_pairs={{7,0},{0,1},{1,2},{2,3},{3,4},{4,5},{5,6},{6,7},{15,8},{8,9},{9,10... | collective-permute-start | bytes 98312 | tf_op jit(solution)/shard_map/while/body/eval_jaxpr/ppermute | solution.py:14
  39.1 4.3 %collective-permute-start = (bf16[2,32,256]{2,1,0:T(8,128)(2,1)S(1)}, bf16[2,32,256]{2,1,0:T(8,128)(2,1)S(1)}, u32[]{:S(2)}, u32[]{:S(2)}) collective-permute-start(bf16[2,32,256]{2,1,0:T(8,128)(2,1)S(1)} %get-tuple-element.449), channel_id=1, source_target_pairs={{7,0},{0,1},{1,2},{2,3},{3,4},{4,5},{5,6},{6,7},{15,8},{8,9},{9,10... | collective-permute-start | bytes 98312 | tf_op jit(solution)/shard_map/while/body/eval_jaxpr/ppermute | solution.py:14
  43.6 4.3 %collective-permute-start = (bf16[2,32,256]{2,1,0:T(8,128)(2,1)S(1)}, bf16[2,32,256]{2,1,0:T(8,128)(2,1)S(1)}, u32[]{:S(2)}, u32[]{:S(2)}) collective-permute-start(bf16[2,32,256]{2,1,0:T(8,128)(2,1)S(1)} %get-tuple-element.449), channel_id=1, source_target_pairs={{7,0},{0,1},{1,2},{2,3},{3,4},{4,5},{5,6},{6,7},{15,8},{8,9},{9,10... | collective-permute-start | bytes 98312 | tf_op jit(solution)/shard_map/while/body/eval_jaxpr/ppermute | solution.py:14
  52.6 1.6 copy-start.3
  55.0 1.3 copy-start.4
  58.9 1.6 copy-start.3
  61.2 1.3 copy-start.4
  62.5 30.2 %all-to-all-start = ((bf16[256,32,128]{2,1,0:T(8,128)(2,1)}), bf16[256,32,128]{2,1,0:T(8,128)(2,1)S(1)}, u32[]{:S(2)}, u32[]{:S(2)}) async-start(bf16[256,32,128]{2,1,0:T(8,128)(2,1)} %bitcast.132), calls=%async_computation | async-start | bytes 4194304 | tf_op jit(solution)/shard_map/all_to_all | solution.py:73
  66.1 155.6 %reduce-scatter.2.cloned.1.call-start = ((), (), s32[]{:S(2)}) async-start(), calls=%async_computation.3 | async-start | bytes 294912 | tf_op jit(solution)/shard_map/reduce_scatter | solution.py:94
  92.7 1.3 copy-start.2
  189.0 0.7 copy-start
Sparse Core Ops, SparseCore 0:
  11.0 152.3 all-gather.1
  189.8 31.8 reduce-scatter.1
where the time goes:
time: 229 us
  waiting for transfers between devices  155 us (68%)
  local copies, waits for them, and re-layouts  31.3 us (14%)
  between operations  13.6 us (6%)
  matrix products  12.7 us (6%)
  other arithmetic  6.8 us (3%)
  starting transfers between devices  4.5 us (2%)
  loops' own time  4.39 us (2%)
    all_gather x1, waiting for transfers between devices, per_device(): all_tensor = lax.all_gather(tensor_eff, 'ri', axis=0, tiled=True)  67.1 us
    reduce_scatter x1, waiting for transfers between devices, per_device(): lax.psum_scatter(lax.fori_loop(0, piece_count, add_piece, jnp.zeros((pola...  32 us
    ppermute x7, waiting for transfers between devices, shifted(): return lax.ppermute(block, axis, route)  29.6 us
    all_to_all x1, waiting for transfers between devices, per_device(): lax.all_to_all(half_occ, 'ao', split_axis=0, concat_axis=1, tiled=True)  26.5 us
    all_gather x1, local copies, waits for them, and re-layouts, per_device(): all_tensor = lax.all_gather(tensor_eff, 'ri', axis=0, tiled=True)  13.8 us
    dot_general x2, matrix products, add_piece(): jnp.einsum('qln,lnp->qp', virt_part, occ_part, preferred_element_type=jnp...  11.8 us
    unnamed x17, local copies, waits for them, and re-layouts  6.7 us
    while x15, local copies, waits for them, and re-layouts  4.9 us
  transfers between devices with their start and end apart: 10, of which 10 were waited for; matrix products, arithmetic and copies ran while one was open for 5% of the time, Pallas kernels for 0%

commit v1 on v0

--- a/solution.py
+++ b/solution.py
@@ -70,7 +70,10 @@
     half_occ = lax.map(occ_piece, jnp.arange(piece_count, dtype=jnp.int32)).reshape(
         ao_total, own_width, own_rows
     )
-    half_occ_local = lax.all_to_all(half_occ, "ao", split_axis=0, concat_axis=1, tiled=True)
+    half_occ_local = jnp.concatenate(
+        lax.all_to_all(jnp.stack(jnp.split(half_occ, lax.axis_size("ao"), axis=0)), "ao", 0, 0),
+        axis=1,
+    )
 
     def virt_piece(source_rows, piece_index):
         columns = lax.dynamic_slice_in_dim(virt_rows, piece_index * span_cols, span_cols, 3)

time: 229 us -> 229 us (level)
  waiting for transfers between devices: 155 us -> 145 us
  local copies, waits for them, and re-layouts: 31.3 us -> 41 us
    all_gather x1, waiting for transfers between devices: 67.1 us -> 57.3 us  [per_device(): all_tensor = lax.all_gather(tensor_eff, 'ri', axis=0, tiled=True)]
    unnamed x17 -> x26, local copies, waits for them, and re-layouts: 6.7 us -> 15.7 us
  transfers between devices with their start and end apart: 10 -> 10, of which waited for: 10 -> 10; matrix products, arithmetic and copies ran while one was open for 5% -> 10% of each run, Pallas kernels for 0% -> 0%
where the time goes in v1:
time: 229 us
  waiting for transfers between devices  145 us (63%)
  local copies, waits for them, and re-layouts  41 us (18%)
  between operations  13.6 us (6%)
  matrix products  12.7 us (6%)
  other arithmetic  6.8 us (3%)
  starting transfers between devices  4.5 us (2%)
  loops' own time  4.39 us (2%)
    all_gather x1, waiting for transfers between devices, per_device(): all_tensor = lax.all_gather(tensor_eff, 'ri', axis=0, tiled=True)  57.3 us
    reduce_scatter x1, waiting for transfers between devices, per_device(): lax.psum_scatter(lax.fori_loop(0, piece_count, add_piece, jnp.zeros((pola...  32 us
    ppermute x7, waiting for transfers between devices, shifted(): return lax.ppermute(block, axis, route)  29.6 us
    all_to_all x1, waiting for transfers between devices, per_device(): lax.all_to_all(jnp.stack(jnp.split(half_occ, lax.axis_size('ao'), axis=0)...  26.5 us
    unnamed x26, local copies, waits for them, and re-layouts  15.7 us
    all_gather x1, local copies, waits for them, and re-layouts, per_device(): all_tensor = lax.all_gather(tensor_eff, 'ri', axis=0, tiled=True)  13.8 us
    dot_general x2, matrix products, add_piece(): jnp.einsum('qln,lnp->qp', virt_part, occ_part, preferred_element_type=jnp...  11.8 us
    while x15, local copies, waits for them, and re-layouts  4.92 us
  transfers between devices with their start and end apart: 10, of which 10 were waited for; matrix products, arithmetic and copies ran while one was open for 10% of the time, Pallas kernels for 0%

profile of v1, /device:TPU:0, one launch (start us, length us, event | category | flops | bytes accessed | tf_op | source)
XLA Modules:
  0.0 228.5 jit_solution(676546712682296193)
XLA Ops:
  6.5 0.7 convert_element_type.41
  7.7 3.1 %broadcast_multiply_fusion.1 = bf16[128,32,256]{2,1,0:T(8,128)(2,1)} fusion(bf16[128,32,256]{2,1,0:T(8,128)(2,1)} %param.13, bf16[128,256]{1,0:T(8,128)(2,1)S(1)} %copy.48), kind=kLoop, calls=%fused_computation.23 | loop fusion | flops 1048576 | bytes 4259840 | tf_op jit(solution)/shard_map/mul | solution.py:39
  10.9 1.6 copy-done.1
  12.5 3.1 %copy.50 = bf16[128,32,256]{0,2,1:T(8,128)(2,1)} copy(bf16[128,32,256]{2,1,0:T(8,128)(2,1)S(1)} %copy-done.1) | data formatting | bytes 4194304 | tf_op args[0]
  16.1 32.0 %while.41 = (s32[]{:T(128)}, bf16[2,32,256]{2,1,0:T(8,128)(2,1)S(1)}, f32[2,1,8,32,256]{4,3,2,1,0:T(8,128)S(1)}, s32[]{:T(128)}, s32[1,8]{1,0:T(1,128)S(1)}, /*index=5*/s32[]{:T(128)}, s32[]{:T(128)}, s32[]{:T(128)}, s32[]{:T(128)}) while((s32[]{:T(128)}, bf16[2,32,256]{2,1,0:T(8,128)(2,1)S(1)}, f32[2,1,8,32,256]{4,3,2,1,0:T(8,128)S(1)}, ...), condition=%wide.region_1.2_spmd, body=%wide.region_0.1_spmd.sunk | while | flops 278559 | bytes 1409390 | solution.py:54
  16.1 0.5 collective-permute-start
  16.6 4.5 %collective-permute-done = bf16[2,32,256]{2,1,0:T(8,128)(2,1)S(1)} collective-permute-done((bf16[2,32,256]{2,1,0:T(8,128)(2,1)S(1)}, bf16[2,32,256]{2,1,0:T(8,128)(2,1)S(1)}, u32[]{:S(2)}, u32[]{:S(2)}) %collective-permute-start) | collective-permute-done | bytes 32800 | tf_op jit(solution)/shard_map/while/body/eval_jaxpr/ppermute | solution.py:14
  21.1 0.1 bitcast_add_fusion.2
  21.4 4.2 %collective-permute-done = bf16[2,32,256]{2,1,0:T(8,128)(2,1)S(1)} collective-permute-done((bf16[2,32,256]{2,1,0:T(8,128)(2,1)S(1)}, bf16[2,32,256]{2,1,0:T(8,128)(2,1)S(1)}, u32[]{:S(2)}, u32[]{:S(2)}) %collective-permute-start) | collective-permute-done | bytes 32800 | tf_op jit(solution)/shard_map/while/body/eval_jaxpr/ppermute | solution.py:14
  25.6 0.1 bitcast_add_fusion.2
  25.8 4.2 %collective-permute-done = bf16[2,32,256]{2,1,0:T(8,128)(2,1)S(1)} collective-permute-done((bf16[2,32,256]{2,1,0:T(8,128)(2,1)S(1)}, bf16[2,32,256]{2,1,0:T(8,128)(2,1)S(1)}, u32[]{:S(2)}, u32[]{:S(2)}) %collective-permute-start) | collective-permute-done | bytes 32800 | tf_op jit(solution)/shard_map/while/body/eval_jaxpr/ppermute | solution.py:14
  30.0 0.1 bitcast_add_fusion.2
  30.3 4.2 %collective-permute-done = bf16[2,32,256]{2,1,0:T(8,128)(2,1)S(1)} collective-permute-done((bf16[2,32,256]{2,1,0:T(8,128)(2,1)S(1)}, bf16[2,32,256]{2,1,0:T(8,128)(2,1)S(1)}, u32[]{:S(2)}, u32[]{:S(2)}) %collective-permute-start) | collective-permute-done | bytes 32800 | tf_op jit(solution)/shard_map/while/body/eval_jaxpr/ppermute | solution.py:14
  34.5 0.1 bitcast_add_fusion.2
  34.8 4.2 %collective-permute-done = bf16[2,32,256]{2,1,0:T(8,128)(2,1)S(1)} collective-permute-done((bf16[2,32,256]{2,1,0:T(8,128)(2,1)S(1)}, bf16[2,32,256]{2,1,0:T(8,128)(2,1)S(1)}, u32[]{:S(2)}, u32[]{:S(2)}) %collective-permute-start) | collective-permute-done | bytes 32800 | tf_op jit(solution)/shard_map/while/body/eval_jaxpr/ppermute | solution.py:14
  39.2 4.2 %collective-permute-done = bf16[2,32,256]{2,1,0:T(8,128)(2,1)S(1)} collective-permute-done((bf16[2,32,256]{2,1,0:T(8,128)(2,1)S(1)}, bf16[2,32,256]{2,1,0:T(8,128)(2,1)S(1)}, u32[]{:S(2)}, u32[]{:S(2)}) %collective-permute-start) | collective-permute-done | bytes 32800 | tf_op jit(solution)/shard_map/while/body/eval_jaxpr/ppermute | solution.py:14
  43.7 4.2 %collective-permute-done = bf16[2,32,256]{2,1,0:T(8,128)(2,1)S(1)} collective-permute-done((bf16[2,32,256]{2,1,0:T(8,128)(2,1)S(1)}, bf16[2,32,256]{2,1,0:T(8,128)(2,1)S(1)}, u32[]{:S(2)}, u32[]{:S(2)}) %collective-permute-start) | collective-permute-done | bytes 32800 | tf_op jit(solution)/shard_map/while/body/eval_jaxpr/ppermute | solution.py:14
  48.4 1.7 broadcast_multiply_fusion
  50.1 12.4 %while.42 = (s32[]{:T(128)}, bf16[2,128,32,128]{3,2,1,0:T(8,128)(2,1)}, s32[2]{0:T(128)S(1)}, bf16[1,8,32,2,128]{4,2,1,3,0:T(8,128)(2,1)S(1)}, bf16[128,1,32,8,3...) while((s32[]{:T(128)}, bf16[2,128,32,128]{3,2,1,0:T(8,128)(2,1)}, s32[2]{0:T(128)S(1)}, ...), condition=%wide.region_3.4_spmd, body=%wide.region_2.3_spmd.sunk | while | flops 268959744 | bytes 22085836 | solution.py:70
  50.1 0.6 dynamic_slice.40
  52.7 0.5 fusion.60
  53.1 1.1 copy-done.3
  54.3 0.7 copy_dynamic-update-slice_fusion.2
  55.0 1.3 copy-done.4
  56.4 0.6 dynamic_slice.40
  58.9 0.5 fusion.60
  59.4 1.1 copy-done.3
  60.5 0.7 copy_dynamic-update-slice_fusion.2
  61.2 1.3 copy-done.4
  62.6 1.8 fusion.44
  64.4 1.7 fusion.43
  66.1 1.7 fusion.42
  67.8 1.7 fusion.41
  69.4 0.7 fusion.40
  70.2 0.7 fusion.39
  70.9 0.7 fusion.38
  71.6 0.7 fusion.37
  72.3 3.6 %all-to-all-start = ((bf16[8,32,32,128]{3,2,1,0:T(8,128)(2,1)}), bf16[8,32,32,128]{3,2,1,0:T(8,128)(2,1)S(1)}, u32[]{:S(2)}, u32[]{:S(2)}) async-start(bf16[8,32,32,128]{3,2,1,0:T(8,128)(2,1)} %fusion.37), calls=%async_computation | async-start | bytes 4194304 | tf_op jit(solution)/shard_map/all_to_all | solution.py:74
  76.0 26.5 %all-to-all-done = bf16[8,32,32,128]{3,2,1,0:T(8,128)(2,1)S(1)} async-done(((bf16[8,32,32,128]{3,2,1,0:T(8,128)(2,1)}), bf16[8,32,32,128]{3,2,1,0:T(8,128)(2,1)S(1)}, u32[]{:S(2)}, u32[]{:S(2)}) %all-to-all-start) | async-done | bytes 2097184 | tf_op jit(solution)/shard_map/all_to_all | solution.py:74
  102.5 1.3 copy-done.2
  103.8 2.2 copy.54
  106.0 57.3 %all-gather.2.cloned.1.call-done = bf16[512,32,256]{2,1,0:T(8,128)(2,1)} async-done(((bf16[128,32,256]{2,1,0:T(8,128)(2,1)}), bf16[512,32,256]{2,1,0:T(8,128)(2,1)}) %all-gather.2.cloned.1.call-update) | async-done | bytes 8388624 | tf_op jit(solution)/shard_map/all_gather | solution.py:85
  163.4 13.8 %copy.49 = bf16[512,32,256]{0,2,1:T(8,128)(2,1)} copy(bf16[512,32,256]{2,1,0:T(8,128)(2,1)} %all-gather.2.cloned.1.call-done) | data formatting | bytes 16777216 | tf_op jit(solution)/shard_map/all_gather | solution.py:85
  177.2 11.8 %while.43 = (s32[]{:T(128)}, f32[512,128]{1,0:T(8,128)S(1)}, bf16[1,8,32,256]{3,2,1,0:T(8,128)(2,1)S(1)}, bf16[512,1,32,8,32]{0,4,3,2,1:T(8,128)(2,1)}, bf16[32,...) while((s32[]{:T(128)}, f32[512,128]{1,0:T(8,128)S(1)}, ...), condition=%wide.region_5.6_spmd.clone, body=%wide.region_4.5_spmd.clone.sunk | while | flops 1612840960 | bytes 10028700 | solution.py:98
  177.2 5.9 %fusion.65 = f32[512,128]{1,0:T(8,128)S(1)} fusion(bf16[512,1,32,8,32]{0,4,3,2,1:T(8,128)(2,1)} %get-tuple-element.511, bf16[32,256,128]{2,1,0:T(8,128)(2,1)S(1)} %get-tuple-element.512, s32[]{:T(128)S(6)} %select_n.38, f32[512,128]{1,0:T(8,128)S(1)} %get-tuple-element.500, pred[]{:T(512)S(6)} %compare.4, ...), kind=kOutput, calls=%fused_computation.17.clone.1 | convolution fusion | flops 1612840960 | bytes 10028544 | tf_op jit(solution)/shard_map/while/body/eval_jaxpr/qln,lnp->qp/dot_general | solution.py:93
  183.1 5.9 %fusion.65 = f32[512,128]{1,0:T(8,128)S(1)} fusion(bf16[512,1,32,8,32]{0,4,3,2,1:T(8,128)(2,1)} %get-tuple-element.511, bf16[32,256,128]{2,1,0:T(8,128)(2,1)S(1)} %get-tuple-element.512, s32[]{:T(128)S(6)} %select_n.38, f32[512,128]{1,0:T(8,128)S(1)} %get-tuple-element.500, pred[]{:T(512)S(6)} %compare.4, ...), kind=kOutput, calls=%fused_computation.17.clone.1 | convolution fusion | flops 1612840960 | bytes 10028544 | tf_op jit(solution)/shard_map/while/body/eval_jaxpr/qln,lnp->qp/dot_general | solution.py:93
  189.0 0.7 copy-done
  189.7 32.0 %reduce-scatter.2.cloned.1.call-done = f32[64,128]{1,0:T(8,128)} async-done(((f32[512,128]{1,0:T(8,128)}), f32[64,128]{1,0:T(8,128)}) %reduce-scatter.2.cloned.1.call-update) | async-done | bytes 32784 | tf_op jit(solution)/shard_map/reduce_scatter | solution.py:97
  (76 shorter events, 2.2 us)
Async XLA Ops:
  6.5 156.8 %all-gather.2.cloned.1.call-start = ((), (), s32[]{:S(2)}) async-start(), calls=%async_computation.2 | async-start | bytes 10485760 | tf_op jit(solution)/shard_map/all_gather | solution.py:85
  10.8 1.6 copy-start.1
  12.4 3.1 %copy-start.8 = (s32[1,8]{1,0:T(1,128)S(1)}, s32[1,8]{1,0:T(1,128)}, u32[]{:S(2)}) copy-start(s32[1,8]{1,0:T(1,128)} %param.18) | copy-start | bytes 100
  12.4 3.3 %copy-start.9 = (s32[1,8]{1,0:T(1,128)S(1)}, s32[1,8]{1,0:T(1,128)}, u32[]{:S(2)}) copy-start(s32[1,8]{1,0:T(1,128)} %param.17) | copy-start | bytes 100
  12.4 3.5 %copy-start.6 = (bf16[32,256]{1,0:T(8,128)(2,1)S(1)}, bf16[32,256]{1,0:T(8,128)(2,1)}, u32[]{:S(2)}) copy-start(bf16[32,256]{1,0:T(8,128)(2,1)} %param.16) | copy-start | bytes 49156
  12.4 3.5 %copy-start.7 = (bf16[32,256]{1,0:T(8,128)(2,1)S(1)}, bf16[32,256]{1,0:T(8,128)(2,1)}, u32[]{:S(2)}) copy-start(bf16[32,256]{1,0:T(8,128)(2,1)} %param.15) | copy-start | bytes 49156
  12.4 3.5 %copy-start.10 = (s32[1,8]{1,0:T(1,128)S(1)}, s32[1,8]{1,0:T(1,128)}, u32[]{:S(2)}) copy-start(s32[1,8]{1,0:T(1,128)} %param.19) | copy-start | bytes 100
  16.1 5.0 %collective-permute-start = (bf16[2,32,256]{2,1,0:T(8,128)(2,1)S(1)}, bf16[2,32,256]{2,1,0:T(8,128)(2,1)S(1)}, u32[]{:S(2)}, u32[]{:S(2)}) collective-permute-start(bf16[2,32,256]{2,1,0:T(8,128)(2,1)S(1)} %get-tuple-element.449), channel_id=1, source_target_pairs={{7,0},{0,1},{1,2},{2,3},{3,4},{4,5},{5,6},{6,7},{15,8},{8,9},{9,10... | collective-permute-start | bytes 98312 | tf_op jit(solution)/shard_map/while/body/eval_jaxpr/ppermute | solution.py:14
  21.3 4.3 %collective-permute-start = (bf16[2,32,256]{2,1,0:T(8,128)(2,1)S(1)}, bf16[2,32,256]{2,1,0:T(8,128)(2,1)S(1)}, u32[]{:S(2)}, u32[]{:S(2)}) collective-permute-start(bf16[2,32,256]{2,1,0:T(8,128)(2,1)S(1)} %get-tuple-element.449), channel_id=1, source_target_pairs={{7,0},{0,1},{1,2},{2,3},{3,4},{4,5},{5,6},{6,7},{15,8},{8,9},{9,10... | collective-permute-start | bytes 98312 | tf_op jit(solution)/shard_map/while/body/eval_jaxpr/ppermute | solution.py:14
  25.7 4.3 %collective-permute-start = (bf16[2,32,256]{2,1,0:T(8,128)(2,1)S(1)}, bf16[2,32,256]{2,1,0:T(8,128)(2,1)S(1)}, u32[]{:S(2)}, u32[]{:S(2)}) collective-permute-start(bf16[2,32,256]{2,1,0:T(8,128)(2,1)S(1)} %get-tuple-element.449), channel_id=1, source_target_pairs={{7,0},{0,1},{1,2},{2,3},{3,4},{4,5},{5,6},{6,7},{15,8},{8,9},{9,10... | collective-permute-start | bytes 98312 | tf_op jit(solution)/shard_map/while/body/eval_jaxpr/ppermute | solution.py:14
  30.2 4.3 %collective-permute-start = (bf16[2,32,256]{2,1,0:T(8,128)(2,1)S(1)}, bf16[2,32,256]{2,1,0:T(8,128)(2,1)S(1)}, u32[]{:S(2)}, u32[]{:S(2)}) collective-permute-start(bf16[2,32,256]{2,1,0:T(8,128)(2,1)S(1)} %get-tuple-element.449), channel_id=1, source_target_pairs={{7,0},{0,1},{1,2},{2,3},{3,4},{4,5},{5,6},{6,7},{15,8},{8,9},{9,10... | collective-permute-start | bytes 98312 | tf_op jit(solution)/shard_map/while/body/eval_jaxpr/ppermute | solution.py:14
  34.7 4.3 %collective-permute-start = (bf16[2,32,256]{2,1,0:T(8,128)(2,1)S(1)}, bf16[2,32,256]{2,1,0:T(8,128)(2,1)S(1)}, u32[]{:S(2)}, u32[]{:S(2)}) collective-permute-start(bf16[2,32,256]{2,1,0:T(8,128)(2,1)S(1)} %get-tuple-element.449), channel_id=1, source_target_pairs={{7,0},{0,1},{1,2},{2,3},{3,4},{4,5},{5,6},{6,7},{15,8},{8,9},{9,10... | collective-permute-start | bytes 98312 | tf_op jit(solution)/shard_map/while/body/eval_jaxpr/ppermute | solution.py:14
  39.1 4.3 %collective-permute-start = (bf16[2,32,256]{2,1,0:T(8,128)(2,1)S(1)}, bf16[2,32,256]{2,1,0:T(8,128)(2,1)S(1)}, u32[]{:S(2)}, u32[]{:S(2)}) collective-permute-start(bf16[2,32,256]{2,1,0:T(8,128)(2,1)S(1)} %get-tuple-element.449), channel_id=1, source_target_pairs={{7,0},{0,1},{1,2},{2,3},{3,4},{4,5},{5,6},{6,7},{15,8},{8,9},{9,10... | collective-permute-start | bytes 98312 | tf_op jit(solution)/shard_map/while/body/eval_jaxpr/ppermute | solution.py:14
  43.6 4.3 %collective-permute-start = (bf16[2,32,256]{2,1,0:T(8,128)(2,1)S(1)}, bf16[2,32,256]{2,1,0:T(8,128)(2,1)S(1)}, u32[]{:S(2)}, u32[]{:S(2)}) collective-permute-start(bf16[2,32,256]{2,1,0:T(8,128)(2,1)S(1)} %get-tuple-element.449), channel_id=1, source_target_pairs={{7,0},{0,1},{1,2},{2,3},{3,4},{4,5},{5,6},{6,7},{15,8},{8,9},{9,10... | collective-permute-start | bytes 98312 | tf_op jit(solution)/shard_map/while/body/eval_jaxpr/ppermute | solution.py:14
  52.7 1.6 copy-start.3
  55.0 1.3 copy-start.4
  58.9 1.6 copy-start.3
  61.2 1.3 copy-start.4
  62.6 6.9 %copy-start.5 = (bf16[2,128,32,128]{3,2,1,0:T(8,128)(2,1)S(1)}, bf16[2,128,32,128]{3,2,1,0:T(8,128)(2,1)}, u32[]{:S(2)}) copy-start(bf16[2,128,32,128]{3,2,1,0:T(8,128)(2,1)} %get-tuple-element.260) | copy-start | bytes 6291460
  72.3 30.2 %all-to-all-start = ((bf16[8,32,32,128]{3,2,1,0:T(8,128)(2,1)}), bf16[8,32,32,128]{3,2,1,0:T(8,128)(2,1)S(1)}, u32[]{:S(2)}, u32[]{:S(2)}) async-start(bf16[8,32,32,128]{3,2,1,0:T(8,128)(2,1)} %fusion.37), calls=%async_computation | async-start | bytes 4194304 | tf_op jit(solution)/shard_map/all_to_all | solution.py:74
  75.9 145.8 %reduce-scatter.2.cloned.1.call-start = ((), (), s32[]{:S(2)}) async-start(), calls=%async_computation.3 | async-start | bytes 294912 | tf_op jit(solution)/shard_map/reduce_scatter | solution.py:97
  102.5 1.3 copy-start.2
  189.0 0.7 copy-start
Sparse Core Ops, SparseCore 0:
  11.0 152.3 all-gather.1
  189.8 31.8 reduce-scatter.1
